TPU v7x, 32 devices: a whole 2x2x4 slice. The times are simulated.
32 devices in a mesh: groups: 2 (over y), inner: 16 (over z, x, core).
Axes of the slice: x: 2, y: 2, z: 4, core: 2. Of those that a mesh axis runs over, the one named last changes fastest.
Arguments:
- ticks: bfloat16 [262144, 128], P(('groups', 'inner')), parts along dimension 0, may hold values from -6 to 6
- conv_weight: bfloat16 [2048, 768], replicated, may hold values from -0.125 to 0.125
- norm_gain: float32 [768], replicated, may hold values from 0.25 to 1.75
- qkv_weight: bfloat16 [768, 2304], replicated, may hold values from -0.21875 to 0.21875
- head_gain: float32 [768], replicated, may hold values from 0.25 to 1.75
- out_weight: bfloat16 [768, 768], replicated, may hold values from -0.21875 to 0.21875
- state_in: float32 [24, 64, 64], P('groups'), parts along dimension 0, may hold values from -768 to 768
Outputs:
- layer_out: bfloat16 [32768, 768], P(('groups', 'inner')), parts along dimension 0
There are 2 independent parts, one for each index of `groups`. A program takes and returns all parts, laid end to end along the dimension named above; an argument that names none is the same for every part. Nothing has to cross between parts.
All inputs are finite; a program needn't handle non-finite values.
Results may differ from a plain program's by a relative error of at most 0.008.
Values may be sent and summed in bfloat16 or wider, within the bound.
No kernel may reach another device: no remote copies, remote signals or barrier semaphores. Data moves between devices by JAX's collectives and lax.ppermute only.
A program may use at most 192 MiB of HBM per device.

v0:
```python
import jax
import jax.numpy as jnp
from jax import lax
from jax.sharding import PartitionSpec as P

STRIDE = 8
BLK = 512


def from_behind(value, axis, steps):
    count = lax.axis_size(axis)
    initial, last = (max(0, -steps), min(count, count - steps))
    return lax.ppermute(value, axis, [(source, source + steps) for source in range(initial, last)])


def shards(ticks, conv_weight, norm_gain, qkv_weight, head_gain, out_weight, state_in):
    row_width = STRIDE * ticks.shape[1]
    token_count = ticks.shape[0] // STRIDE
    tick_rows = ticks.reshape(token_count, row_width)
    weight_prev = conv_weight[:row_width]
    current = jnp.dot(tick_rows, conv_weight[row_width:], preferred_element_type=jnp.float32)
    last_row = from_behind(tick_rows[token_count - 1 :], "inner", 1)
    earlier_rows = jnp.concatenate([last_row, tick_rows[:-1]], 0)
    embedded_f = current + jnp.dot(earlier_rows, weight_prev, preferred_element_type=jnp.float32)
    embedded = embedded_f.astype(jnp.bfloat16)
    embed_f = embedded.astype(jnp.float32)
    normed = (
        embed_f * lax.rsqrt(jnp.mean(embed_f * embed_f, -1, keepdims=True) + 1e-05) * norm_gain
    ).astype(jnp.bfloat16)
    qkv = jnp.dot(normed, qkv_weight, preferred_element_type=jnp.float32).astype(jnp.bfloat16)
    model_width = embedded.shape[1]
    head_count = state_in.shape[0]
    head_size = state_in.shape[1]
    block_count = token_count // BLK
    queries = qkv[:, :model_width].reshape(block_count, BLK, head_count, head_size)
    keys_all = qkv[:, model_width : 2 * model_width].reshape(
        block_count, BLK, head_count, head_size
    )
    values_all = qkv[:, 2 * model_width :].reshape(block_count, BLK, head_count, head_size)
    block_states = jnp.einsum(
        "bthi,bthj->bhij", keys_all, values_all, preferred_element_type=jnp.float32
    )
    local_state = jnp.sum(block_states, 0)
    every_state = lax.all_gather(local_state[None], "inner", axis=0, tiled=True)
    lower_dev = (jnp.arange(every_state.shape[0]) < lax.axis_index("inner")).astype(jnp.float32)
    prefix = jnp.einsum("n,nhij->hij", lower_dev, every_state, precision=lax.Precision.HIGHEST)
    carried = state_in + prefix
    within = jnp.cumsum(block_states, 0) - block_states
    state_before = carried[None] + within
    lower = jnp.arange(BLK)[:, None] >= jnp.arange(BLK)[None, :]
    scores = jnp.einsum("bthd,bshd->bhts", queries, keys_all, preferred_element_type=jnp.float32)
    scores = jnp.where(lower[None, None], scores, 0.0).astype(jnp.bfloat16)
    inside_term = jnp.einsum(
        "bhts,bshd->bthd", scores, values_all, preferred_element_type=jnp.float32
    )
    carried_term = jnp.einsum(
        "bthi,bhij->bthj",
        queries.astype(jnp.float32),
        state_before,
        precision=lax.Precision.HIGHEST,
    )
    combined = (inside_term + carried_term).reshape(token_count, head_count, head_size)
    attended = (
        combined
        * lax.rsqrt(jnp.mean(combined * combined, -1, keepdims=True) + 1e-06)
        * head_gain.reshape(head_count, head_size)
    )
    attended = attended.reshape(token_count, model_width).astype(jnp.bfloat16)
    return (embed_f + jnp.dot(attended, out_weight, preferred_element_type=jnp.float32)).astype(
        jnp.bfloat16
    )


def solution(mesh):
    in_specs = (P(("groups", "inner"), None), P(), P(), P(), P(), P(), P("groups", None, None))
    out_specs = P(("groups", "inner"), None)
    return jax.shard_map(shards, mesh=mesh, in_specs=in_specs, out_specs=out_specs, check_vma=False)
```

profile of v0, /device:TPU:0, one launch (start us, length us, event | category | flops | bytes accessed | tf_op | source)
XLA Modules:
  0.0 145.3 jit_solution(13970756868127508273)
XLA Ops:
  6.5 0.8 slice_bitcast_fusion
  7.4 2.5 %collective-permute-start = (bf16[1,1024]{1,0:T(2,128)(2,1)S(1)}, bf16[1,1024]{1,0:T(2,128)(2,1)S(1)}, u32[]{:S(2)}, u32[]{:S(2)}) collective-permute-start(bf16[1,1024]{1,0:T(2,128)(2,1)S(1)} %bitcast.53), channel_id=1, source_target_pairs={{0,1},{1,2},{2,3},{3,4},{4,5},{5,6},{6,7},{7,8},{8,9},{9,10},{10,1... | collective-permute-start | bytes 6152 | tf_op jit(solution)/shard_map/ppermute | solution.py:13
  9.9 4.2 %reshape.62 = bf16[1024,1024]{1,0:T(8,128)(2,1)} reshape(bf16[8192,128]{1,0:T(8,128)(2,1)} %param.7) | data formatting | bytes 4194304 | tf_op jit(solution)/shard_map/reshape | solution.py:19
  14.0 5.7 %fusion.21 = f32[1024,768]{0,1:T(8,128)} fusion(bf16[1024,1024]{1,0:T(8,128)(2,1)} %reshape.62, bf16[2048,768]{1,0:T(8,128)(2,1)} %param.8), kind=kOutput, calls=%fused_computation.28 | convolution fusion | flops 1610612736 | bytes 6815744 | tf_op jit(solution)/shard_map/dot_general | solution.py:21
  19.7 1.5 %slice.30 = bf16[8184,128]{1,0:T(8,128)(2,1)} slice(bf16[8192,128]{1,0:T(8,128)(2,1)S(1)} %copy-done.2), slice={[0:8184], [0:128]} | slice | bytes 4190208 | tf_op jit(solution)/shard_map/slice | solution.py:23
  21.2 4.2 %slice.31 = bf16[1023,1024]{1,0:T(8,128)(2,1)} reshape(bf16[8184,128]{1,0:T(8,128)(2,1)} %slice.30) | data formatting | bytes 4190208 | tf_op jit(solution)/shard_map/slice | solution.py:23
  25.3 5.0 %fusion.7 = (f32[1024]{0:T(1024)S(1)}, bf16[1024,768]{0,1:T(8,128)(2,1)S(1)}) fusion(f32[1024,768]{0,1:T(8,128)} %fusion.21, bf16[2048,768]{1,0:T(8,128)(2,1)} %param.8, bf16[1023,1024]{1,0:T(8,128)(2,1)} %slice.31, bf16[1,1024]{1,0:T(2,128)(2,1)S(1)} %collective-permute-done), kind=kOutput, calls=%fused_computation.11 | convolution fusion | flops 1618738176 | bytes 8394752 | tf_op jit(solution)/shard_map/dot_general | solution.py:24
  30.4 4.4 %convolution_convert_fusion = bf16[1024,2304]{1,0:T(8,128)(2,1)S(1)} fusion(bf16[768,2304]{1,0:T(8,128)(2,1)S(1)} %copy-done, bf16[1024,768]{0,1:T(8,128)(2,1)S(1)} %get-tuple-element.9, f32[768]{0:T(1024)S(1)} %copy-done.11, f32[1024]{0:T(1024)S(1)} %add_rsqrt_fusion.1), kind=kOutput, calls=%fused_computation.7 | convolution fusion | flops 3629383680 | bytes 9837568 | tf_op jit(solution)/shard_map/dot_general | solution.py:30
  34.8 1.5 %fusion.43 = (bf16[1024,768]{1,0:T(8,128)(2,1)S(1)}, bf16[1024,768]{1,0:T(8,128)(2,1)S(1)}, bf16[1024,768]{1,0:T(8,128)(2,1)}) fusion(bf16[1024,2304]{1,0:T(8,128)(2,1)S(1)} %convolution_convert_fusion), kind=kLoop, calls=%fused_computation.51 | loop fusion | bytes 9437184 | tf_op jit(solution)/shard_map/slice | solution.py:35
  36.2 2.6 %copy.39 = bf16[1024,768]{0,1:T(8,128)(2,1)} copy(bf16[1024,768]{1,0:T(8,128)(2,1)} %get-tuple-element.7) | data formatting | bytes 3145728 | tf_op jit(solution)/shard_map/slice | solution.py:39
  38.8 3.9 %reshape.63 = bf16[2,512,12,64]{1,0,3,2:T(2,128)(2,1)} reshape(bf16[1024,768]{0,1:T(8,128)(2,1)} %copy.39) | data formatting | bytes 3145728 | tf_op jit(solution)/shard_map/reshape | solution.py:39
  42.7 1.7 %copy.41 = bf16[1024,768]{0,1:T(8,128)(2,1)} copy(bf16[1024,768]{1,0:T(8,128)(2,1)S(1)} %get-tuple-element.6) | data formatting | bytes 3145728 | tf_op jit(solution)/shard_map/slice | solution.py:36
  44.4 4.0 %reshape.65 = bf16[2,512,12,64]{1,0,3,2:T(2,128)(2,1)} reshape(bf16[1024,768]{0,1:T(8,128)(2,1)} %copy.41) | data formatting | bytes 3145728 | tf_op jit(solution)/shard_map/reshape | solution.py:36
  48.3 3.7 %fusion.44 = (f32[12,64,64]{2,1,0:T(8,128)}, f32[2,12,64,64]{3,2,1,0:T(8,128)}) fusion(bf16[2,512,12,64]{1,0,3,2:T(2,128)(2,1)S(1)} %copy-done.7, bf16[2,512,12,64]{1,0,3,2:T(2,128)(2,1)} %reshape.65), kind=kOutput, calls=%fused_computation.52 | convolution fusion | flops 100712448 | bytes 3735552 | tf_op jit(solution)/shard_map/bthi,bthj->bhij/dot_general | solution.py:40
  52.9 1.2 reshape.64
  54.1 10.5 %fusion = f32[2,12,64,512]{3,2,1,0:T(8,128)} fusion(pred[512,512]{1,0:T(8,128)(4,1)S(1)} %iota_compare_fusion, bf16[2,512,12,64]{1,0,3,2:T(2,128)(2,1)} %reshape.63, bf16[2,512,12,64]{1,0,3,2:T(2,128)(2,1)} %reshape.65, bf16[2,512,12,64]{1,0,3,2:T(2,128)(2,1)S(1)} %reshape.64), kind=kOutput, calls=%fused_computation.1 | convolution fusion | flops 1623195648 | bytes 8126464 | tf_op jit(solution)/shard_map/bhts,bshd->bthd/dot_general | solution.py:53
  64.6 52.0 %all-gather.3.cloned.1.call-done = f32[192,64,64]{2,1,0:T(8,128)} async-done(((f32[12,64,64]{2,1,0:T(8,128)}), f32[192,64,64]{2,1,0:T(8,128)}) %all-gather.3.cloned.1.call-update) | async-done | bytes 3145744 | tf_op jit(solution)/shard_map/all_gather | solution.py:44
  116.6 8.4 %fusion.5 = f32[1,12,64,64]{3,0,2,1:T(1,128)S(1)} fusion(f32[16,12,64,64]{3,2,1,0:T(8,128)} %bitcast.48, s32[]{:T(128)S(6)} %axis_index.12), kind=kOutput, calls=%fused_computation.5 | convolution fusion | flops 9437200 | bytes 3342340 | tf_op jit(solution)/shard_map/n,nhij->hij/dot_general | solution.py:46
  125.6 0.8 copy-done.4
  126.4 1.7 %multiply_reduce_fusion = (f32[2,512,12]{1,2,0:T(8,128)S(1)}, f32[2,512,12,64]{1,3,2,0:T(8,128)S(1)}) fusion(f32[2,12,64,512]{3,2,1,0:T(8,128)S(1)} %copy-done.5, f32[2,12,64,64]{3,2,1,0:T(8,128)S(1)} %fusion.27, bf16[2,512,12,64]{1,0,3,2:T(2,128)(2,1)S(1)} %copy-done.4), kind=kOutput, calls=%fused_computation.18 | convolution fusion | flops 606326784 | bytes 8306688 | tf_op jit(solution)/shard_map/bthi,bhij->bthj/dot_general | solution.py:56
  128.2 2.4 %copy.49 = f32[2,512,12,64]{1,0,3,2:T(2,128)S(1)} copy(f32[2,512,12,64]{1,3,2,0:T(8,128)S(1)} %get-tuple-element.13) | data formatting | bytes 6291456 | tf_op jit(solution)/shard_map/add | solution.py:62
  131.9 0.9 copy-done.10
  133.3 2.6 %fusion.10 = bf16[1024,768]{0,1:T(8,128)(2,1)} fusion(bf16[1024,768]{0,1:T(8,128)(2,1)S(1)} %copy-done.13, bf16[1024,768]{0,1:T(8,128)(2,1)S(1)} %fusion.12, bf16[768,768]{1,0:T(8,128)(2,1)S(1)} %copy-done.10), kind=kOutput, calls=%fused_computation.14 | convolution fusion | flops 1210318848 | bytes 5898240 | tf_op jit(solution)/shard_map/dot_general | solution.py:69
  135.9 2.6 %copy.52 = bf16[1024,768]{1,0:T(8,128)(2,1)} copy(bf16[1024,768]{0,1:T(8,128)(2,1)} %fusion.10) | data formatting | bytes 3145728 | tf_op jit(solution)/shard_map/convert_element_type | solution.py:69
  (41 shorter events, 3.2 us)
Async XLA Ops:
  6.5 23.8 %copy-start = (bf16[768,2304]{1,0:T(8,128)(2,1)S(1)}, bf16[768,2304]{1,0:T(8,128)(2,1)}, u32[]{:S(2)}) copy-start(bf16[768,2304]{1,0:T(8,128)(2,1)} %param.10) | copy-start | bytes 10616836
  6.5 110.0 %all-gather.3.cloned.1.call-start = ((), (), s32[]{:S(2)}) async-start(), calls=%async_computation | async-start | bytes 6684672 | tf_op jit(solution)/shard_map/all_gather | solution.py:44
  7.4 18.0 %collective-permute-start = (bf16[1,1024]{1,0:T(2,128)(2,1)S(1)}, bf16[1,1024]{1,0:T(2,128)(2,1)S(1)}, u32[]{:S(2)}, u32[]{:S(2)}) collective-permute-start(bf16[1,1024]{1,0:T(2,128)(2,1)S(1)} %bitcast.53), channel_id=1, source_target_pairs={{0,1},{1,2},{2,3},{3,4},{4,5},{5,6},{6,7},{7,8},{8,9},{9,10},{10,1... | collective-permute-start | bytes 6152 | tf_op jit(solution)/shard_map/ppermute | solution.py:13
  14.0 5.7 %copy-start.2 = (bf16[8192,128]{1,0:T(8,128)(2,1)S(1)}, bf16[8192,128]{1,0:T(8,128)(2,1)}, u32[]{:S(2)}) copy-start(bf16[8192,128]{1,0:T(8,128)(2,1)} %param.7) | copy-start | bytes 6291460
  25.3 5.0 %copy-start.11 = (f32[768]{0:T(1024)S(1)}, f32[768]{0:T(1024)}, u32[]{:S(2)}) copy-start(f32[768]{0:T(1024)} %param.9) | copy-start | bytes 9220
  30.3 4.4 %copy-start.12 = (bf16[1024,768]{0,1:T(8,128)(2,1)}, bf16[1024,768]{0,1:T(8,128)(2,1)S(1)}, u32[]{:S(2)}) copy-start(bf16[1024,768]{0,1:T(8,128)(2,1)S(1)} %get-tuple-element.9) | copy-start | bytes 4718596
  44.4 4.0 %copy-start.7 = (bf16[2,512,12,64]{1,0,3,2:T(2,128)(2,1)S(1)}, bf16[2,512,12,64]{1,0,3,2:T(2,128)(2,1)}, u32[]{:S(2)}) copy-start(bf16[2,512,12,64]{1,0,3,2:T(2,128)(2,1)} %reshape.63) | copy-start | bytes 4718596
  54.1 10.5 %copy-start.3 = (bf16[2,512,12,64]{1,0,3,2:T(2,128)(2,1)}, bf16[2,512,12,64]{1,0,3,2:T(2,128)(2,1)S(1)}, u32[]{:S(2)}) copy-start(bf16[2,512,12,64]{1,0,3,2:T(2,128)(2,1)S(1)} %reshape.64) | copy-start | bytes 4718596
  116.6 8.5 %copy-start.8 = (f32[12,64,64]{2,1,0:T(8,128)S(1)}, f32[12,64,64]{2,1,0:T(8,128)}, u32[]{:S(2)}) copy-start(f32[12,64,64]{2,1,0:T(8,128)} %param.13) | copy-start | bytes 589828
  116.6 8.5 %copy-start.6 = (f32[2,12,64,64]{3,2,1,0:T(8,128)S(1)}, f32[2,12,64,64]{3,2,1,0:T(8,128)}, u32[]{:S(2)}) copy-start(f32[2,12,64,64]{3,2,1,0:T(8,128)} %get-tuple-element.11) | copy-start | bytes 1179652
  116.6 9.0 %copy-start.5 = (f32[2,12,64,512]{3,2,1,0:T(8,128)S(1)}, f32[2,12,64,512]{3,2,1,0:T(8,128)}, u32[]{:S(2)}) copy-start(f32[2,12,64,512]{3,2,1,0:T(8,128)} %fusion) | copy-start | bytes 9437188
  125.0 1.4 copy-start.4
  130.6 0.9 copy-start.9
  131.5 1.3 copy-start.10
  131.5 1.8 %copy-start.13 = (bf16[1024,768]{0,1:T(8,128)(2,1)S(1)}, bf16[1024,768]{0,1:T(8,128)(2,1)}, u32[]{:S(2)}) copy-start(bf16[1024,768]{0,1:T(8,128)(2,1)} %copy-done.12) | copy-start | bytes 4718596
  133.3 5.2 %copy-start.1 = (bf16[768,2304]{1,0:T(8,128)(2,1)S(1)}, bf16[768,2304]{1,0:T(8,128)(2,1)}, u32[]{:S(2)}) copy-start(bf16[768,2304]{1,0:T(8,128)(2,1)} %param.10) | copy-start | bytes 10616836
Sparse Core Ops, SparseCore 0:
  52.1 64.4 all-gather.2
where the time goes:
time: 146 us; the launch traced here: 145 us
  waiting for transfers between devices  52 us (36%)
  matrix products  42 us (29%)
  local copies, waits for them, and re-layouts  34.2 us (23%)
  between operations  13.7 us (9%)
  starting transfers between devices  2.48 us (2%)
    all_gather x1, waiting for transfers between devices, shards(): every_state = lax.all_gather(local_state[None], 'inner', axis=0, tiled=True)  52 us
    dot_general x1, matrix products, shards(): jnp.einsum('bhts,bshd->bthd', scores, values_all, preferred_element_type=...  10.5 us
    dot_general x1, matrix products, shards(): jnp.einsum('n,nhij->hij', lower_dev, every_state, precision=lax.Precision...  8.42 us
    dot_general x1, matrix products, shards(): jnp.dot(tick_rows, conv_weight[row_width:], preferred_element_type=jnp.fl...  5.66 us
    slice x2, local copies, waits for them, and re-layouts, shards(): earlier_rows = jnp.concatenate([last_row, tick_rows[:-1]], 0)  5.64 us
    dot_general x1, matrix products, shards(): jnp.dot(earlier_rows, weight_prev, preferred_element_type=jnp.float32)  4.97 us
    dot_general x1, matrix products, shards(): jnp.dot(normed, qkv_weight, preferred_element_type=jnp.float32)  4.36 us
    reshape x1, local copies, waits for them, and re-layouts, shards(): tick_rows = ticks.reshape(token_count, row_width)  4.17 us
  transfers between devices with their start and end apart: 2, of which 1 were waited for; matrix products, arithmetic and copies ran while one was open for 19% of the time, Pallas kernels for 0%

commit v1 on v0

--- a/solution.py
+++ b/solution.py
@@ -5,6 +5,18 @@
 
 STRIDE = 8
 BLK = 512
+
+
+def collect(array, axis, dim):
+    ways, here = (lax.axis_size(axis), lax.axis_index(axis))
+    grown, reach = (array, 1)
+    while reach < ways:
+        theirs = lax.ppermute(grown, axis, [(d, d ^ reach) for d in range(ways)])
+        mine_first = jnp.concatenate([grown, theirs], axis=dim)
+        theirs_first = jnp.concatenate([theirs, grown], axis=dim)
+        grown = jnp.where(here & reach == 0, mine_first, theirs_first)
+        reach = 2 * reach
+    return grown
 
 
 def from_behind(value, axis, steps):
@@ -41,7 +53,7 @@
         "bthi,bthj->bhij", keys_all, values_all, preferred_element_type=jnp.float32
     )
     local_state = jnp.sum(block_states, 0)
-    every_state = lax.all_gather(local_state[None], "inner", axis=0, tiled=True)
+    every_state = collect(local_state[None], "inner", 0)
     lower_dev = (jnp.arange(every_state.shape[0]) < lax.axis_index("inner")).astype(jnp.float32)
     prefix = jnp.einsum("n,nhij->hij", lower_dev, every_state, precision=lax.Precision.HIGHEST)
     carried = state_in + prefix

time: 146 us -> 265 us (1.82)
  waiting for transfers between devices: 52 us -> 169 us
  between operations: 13.7 us -> 0.31 us
  other arithmetic: 1.04 us -> 10.8 us
  starting transfers between devices: 2.48 us -> 11 us
  matrix products: 42 us -> 38.4 us
    ppermute x0 -> x4, waiting for transfers between devices: none -> 169 us  [collect(): theirs = lax.ppermute(grown, axis, [(d, d ^ reach) for d in range(ways)])]
    all_gather x1 -> x0, waiting for transfers between devices: 52 us -> none  [shards(): every_state = lax.all_gather(local_state[None], 'inner', axis=0, tiled=True)]
    ppermute x0 -> x4, starting transfers between devices: none -> 8.54 us  [collect(): theirs = lax.ppermute(grown, axis, [(d, d ^ reach) for d in range(ways)])]
    select_n x0 -> x4, other arithmetic: none -> 7.87 us  [collect(): grown = jnp.where(here & reach == 0, mine_first, theirs_first)]
    reshape x1, local copies, waits for them, and re-layouts: 1.18 us -> 3.85 us  [shards(): qkv[:, :model_width].reshape(block_count, BLK, head_count, head_size)]
  transfers between devices with their start and end apart: 2 -> 5, of which waited for: 1 -> 4; matrix products, arithmetic and copies ran while one was open for 19% -> 13% of each run, Pallas kernels for 0% -> 0%
where the time goes in v1:
time: 265 us; the launch traced here: 264 us
  waiting for transfers between devices  169 us (64%)
  matrix products  38.4 us (14%)
  local copies, waits for them, and re-layouts  34.5 us (13%)
  starting transfers between devices  11 us (4%)
  other arithmetic  10.8 us (4%)
    ppermute x4, waiting for transfers between devices, collect(): theirs = lax.ppermute(grown, axis, [(d, d ^ reach) for d in range(ways)])  169 us
    dot_general x1, matrix products, shards(): jnp.einsum('bhts,bshd->bthd', scores, values_all, preferred_element_type=...  10.2 us
    ppermute x4, starting transfers between devices, collect(): theirs = lax.ppermute(grown, axis, [(d, d ^ reach) for d in range(ways)])  8.54 us
    select_n x4, other arithmetic, collect(): grown = jnp.where(here & reach == 0, mine_first, theirs_first)  7.87 us
    dot_general x1, matrix products, shards(): jnp.einsum('n,nhij->hij', lower_dev, every_state, precision=lax.Precision...  5.99 us
    slice x2, local copies, waits for them, and re-layouts, shards(): earlier_rows = jnp.concatenate([last_row, tick_rows[:-1]], 0)  5.66 us
    dot_general x1, matrix products, shards(): jnp.dot(tick_rows, conv_weight[row_width:], preferred_element_type=jnp.fl...  5.66 us
  transfers between devices with their start and end apart: 5, of which 4 were waited for; matrix products, arithmetic and copies ran while one was open for 13% of the time, Pallas kernels for 0%

profile of v1, /device:TPU:0, one launch (start us, length us, event | category | flops | bytes accessed | tf_op | source)
XLA Modules:
  0.0 264.4 jit_solution(6494431134777391270)
XLA Ops:
  0.8 2.5 collective-permute-start
  3.3 4.2 %reshape.62 = bf16[1024,1024]{1,0:T(8,128)(2,1)} reshape(bf16[8192,128]{1,0:T(8,128)(2,1)} %param.7) | data formatting | bytes 4194304 | tf_op jit(solution)/shard_map/reshape | solution.py:31
  7.5 5.7 %fusion.21 = f32[1024,768]{0,1:T(8,128)} fusion(bf16[1024,1024]{1,0:T(8,128)(2,1)} %reshape.62, bf16[2048,768]{1,0:T(8,128)(2,1)} %param.8), kind=kOutput, calls=%fused_computation.31 | convolution fusion | flops 1610612736 | bytes 6815744 | tf_op jit(solution)/shard_map/dot_general | solution.py:33
  14.7 4.2 %slice.31 = bf16[1023,1024]{1,0:T(8,128)(2,1)} reshape(bf16[8184,128]{1,0:T(8,128)(2,1)} %slice.30) | data formatting | bytes 4190208 | tf_op jit(solution)/shard_map/slice | solution.py:35
  18.8 5.0 %fusion.7 = (f32[1024]{0:T(1024)S(1)}, bf16[1024,768]{0,1:T(8,128)(2,1)S(1)}) fusion(f32[1024,768]{0,1:T(8,128)} %fusion.21, bf16[2048,768]{1,0:T(8,128)(2,1)} %param.8, bf16[1023,1024]{1,0:T(8,128)(2,1)} %slice.31, bf16[1,1024]{1,0:T(2,128)(2,1)S(1)} %collective-permute-done), kind=kOutput, calls=%fused_computation.12 | convolution fusion | flops 1618738176 | bytes 8394752 | tf_op jit(solution)/shard_map/dot_general | solution.py:36
  23.9 4.4 %convolution_convert_fusion = bf16[1024,2304]{1,0:T(8,128)(2,1)S(1)} fusion(bf16[768,2304]{1,0:T(8,128)(2,1)S(1)} %copy-done, bf16[1024,768]{0,1:T(8,128)(2,1)S(1)} %get-tuple-element.9, f32[768]{0:T(1024)S(1)} %copy-done.11, f32[1024]{0:T(1024)S(1)} %add_rsqrt_fusion.1), kind=kOutput, calls=%fused_computation.8 | convolution fusion | flops 3629383680 | bytes 9837568 | tf_op jit(solution)/shard_map/dot_general | solution.py:42
  31.3 3.8 %reshape.65 = bf16[2,512,12,64]{1,0,3,2:T(2,128)(2,1)} reshape(bf16[1024,768]{0,1:T(8,128)(2,1)} %copy.41) | data formatting | bytes 3145728 | tf_op jit(solution)/shard_map/reshape | solution.py:48
  35.9 2.5 reshape.63
  38.4 2.9 %fusion.45 = (f32[12,64,64]{2,1,0:T(8,128)S(1)}, f32[2,12,64,64]{3,2,1,0:T(8,128)}) fusion(bf16[2,512,12,64]{1,0,3,2:T(2,128)(2,1)} %reshape.63, bf16[2,512,12,64]{1,0,3,2:T(2,128)(2,1)S(1)} %copy-done.7), kind=kOutput, calls=%fused_computation.57 | convolution fusion | flops 100712448 | bytes 3735552 | tf_op jit(solution)/shard_map/bthi,bthj->bhij/dot_general | solution.py:52
  41.3 2.6 collective-permute-start.1
  46.9 18.3 %collective-permute-done.2 = f32[2,12,64,64]{3,2,1,0:T(8,128)S(1)} collective-permute-done((f32[2,12,64,64]{3,2,1,0:T(8,128)S(1)}, f32[2,12,64,64]{3,2,1,0:T(8,128)S(1)}, u32[]{:S(2)}, u32[]{:S(2)}) %collective-permute-start.2) | collective-permute-done | bytes 393248 | tf_op jit(solution)/shard_map/ppermute | solution.py:14
  67.1 34.4 %collective-permute-done.3 = f32[4,12,64,64]{3,2,1,0:T(8,128)} collective-permute-done((f32[4,12,64,64]{3,2,1,0:T(8,128)S(1)}, f32[4,12,64,64]{3,2,1,0:T(8,128)}, u32[]{:S(2)}, u32[]{:S(2)}) %collective-permute-start.3) | collective-permute-done | bytes 786464 | tf_op jit(solution)/shard_map/ppermute | solution.py:14
  101.5 3.9 %maximum_select_fusion.1 = f32[8,12,64,64]{3,2,1,0:T(8,128)S(1)} fusion(f32[4,12,64,64]{3,2,1,0:T(8,128)} %collective-permute-done.3, f32[4,12,64,64]{3,2,1,0:T(8,128)} %copy-done.3, pred[]{:T(512)S(6)} %eq.13), kind=kLoop, calls=%fused_computation.16 | loop fusion | flops 1179648 | bytes 3145729 | tf_op jit(solution)/shard_map/jit(_where)/select_n | solution.py:17
  105.4 2.7 %collective-permute-start.4 = (f32[8,12,64,64]{3,2,1,0:T(8,128)S(1)}, f32[8,12,64,64]{3,2,1,0:T(8,128)}, u32[]{:S(2)}, u32[]{:S(2)}) collective-permute-start(f32[8,12,64,64]{3,2,1,0:T(8,128)S(1)} %maximum_select_fusion.1), channel_id=1, source_target_pairs={{0,8},{1,9},{2,10},{3,11},{4,12},{5,13},{6,14},{7,15},{8,0},{9,1},... | collective-permute-start | bytes 4718600 | tf_op jit(solution)/shard_map/ppermute | solution.py:14
  108.2 2.6 copy.40
  110.8 3.9 %reshape.64 = bf16[2,512,12,64]{1,0,3,2:T(2,128)(2,1)} reshape(bf16[1024,768]{0,1:T(8,128)(2,1)} %copy.40) | data formatting | bytes 3145728 | tf_op jit(solution)/shard_map/reshape | solution.py:47
  114.6 2.4 reduce-window_subtract_fusion
  117.0 10.2 %fusion = f32[2,12,64,512]{3,2,1,0:T(8,128)} fusion(pred[512,512]{1,0:T(8,128)(4,1)S(1)} %iota_compare_fusion, bf16[2,512,12,64]{1,0,3,2:T(2,128)(2,1)} %reshape.63, bf16[2,512,12,64]{1,0,3,2:T(2,128)(2,1)} %reshape.65, bf16[2,512,12,64]{1,0,3,2:T(2,128)(2,1)} %reshape.64), kind=kOutput, calls=%fused_computation.1 | convolution fusion | flops 1623195648 | bytes 8126464 | tf_op jit(solution)/shard_map/bhts,bshd->bthd/dot_general | solution.py:65
  127.2 115.4 %collective-permute-done.4 = f32[8,12,64,64]{3,2,1,0:T(8,128)} collective-permute-done((f32[8,12,64,64]{3,2,1,0:T(8,128)S(1)}, f32[8,12,64,64]{3,2,1,0:T(8,128)}, u32[]{:S(2)}, u32[]{:S(2)}) %collective-permute-start.4) | collective-permute-done | bytes 1572896 | tf_op jit(solution)/shard_map/ppermute | solution.py:14
  242.6 3.6 %maximum_select_fusion = f32[16,12,64,64]{3,2,1,0:T(8,128)S(1)} fusion(f32[8,12,64,64]{3,2,1,0:T(8,128)} %collective-permute-done.4, f32[8,12,64,64]{3,2,1,0:T(8,128)S(1)} %maximum_select_fusion.1, pred[]{:T(512)S(6)} %eq.12), kind=kLoop, calls=%fused_computation.5 | loop fusion | flops 2359296 | bytes 6291457 | tf_op jit(solution)/shard_map/jit(_where)/select_n | solution.py:17
  246.2 6.0 %fusion.5 = f32[1,12,64,64]{3,0,2,1:T(1,128)S(1)} fusion(f32[16,12,64,64]{3,2,1,0:T(8,128)S(1)} %maximum_select_fusion, s32[]{:T(128)S(6)} %axis_index.16), kind=kOutput, calls=%fused_computation.6 | convolution fusion | flops 9437200 | bytes 3342340 | tf_op jit(solution)/shard_map/n,nhij->hij/dot_general | solution.py:58
  254.2 2.4 copy.49
  259.1 2.6 fusion.10
  261.8 2.6 copy.52
  (50 shorter events, 15.6 us)
Async XLA Ops:
  0.0 23.8 %copy-start = (bf16[768,2304]{1,0:T(8,128)(2,1)S(1)}, bf16[768,2304]{1,0:T(8,128)(2,1)}, u32[]{:S(2)}) copy-start(bf16[768,2304]{1,0:T(8,128)(2,1)} %param.10) | copy-start | bytes 10616836
  0.8 18.0 %collective-permute-start = (bf16[1,1024]{1,0:T(2,128)(2,1)S(1)}, bf16[1,1024]{1,0:T(2,128)(2,1)S(1)}, u32[]{:S(2)}, u32[]{:S(2)}) collective-permute-start(bf16[1,1024]{1,0:T(2,128)(2,1)S(1)} %bitcast.53), channel_id=1, source_target_pairs={{0,1},{1,2},{2,3},{3,4},{4,5},{5,6},{6,7},{7,8},{8,9},{9,10},{10,1... | collective-permute-start | bytes 6152 | tf_op jit(solution)/shard_map/ppermute | solution.py:25
  7.5 5.7 %copy-start.2 = (bf16[8192,128]{1,0:T(8,128)(2,1)S(1)}, bf16[8192,128]{1,0:T(8,128)(2,1)}, u32[]{:S(2)}) copy-start(bf16[8192,128]{1,0:T(8,128)(2,1)} %param.7) | copy-start | bytes 6291460
  18.8 5.0 %copy-start.11 = (f32[768]{0:T(1024)S(1)}, f32[768]{0:T(1024)}, u32[]{:S(2)}) copy-start(f32[768]{0:T(1024)} %param.9) | copy-start | bytes 9220
  23.8 4.4 %copy-start.12 = (bf16[1024,768]{0,1:T(8,128)(2,1)}, bf16[1024,768]{0,1:T(8,128)(2,1)S(1)}, u32[]{:S(2)}) copy-start(bf16[1024,768]{0,1:T(8,128)(2,1)S(1)} %get-tuple-element.9) | copy-start | bytes 4718596
  35.9 2.5 copy-start.7
  41.3 4.0 %collective-permute-start.1 = (f32[1,12,64,64]{3,2,1,0:T(8,128)S(1)}, f32[1,12,64,64]{3,2,1,0:T(8,128)S(1)}, u32[]{:S(2)}, u32[]{:S(2)}) collective-permute-start(f32[1,12,64,64]{3,2,1,0:T(8,128)S(1)} %bitcast.48), channel_id=1, source_target_pairs={{0,1},{1,0},{2,3},{3,2},{4,5},{5,4},{6,7},{7,6},{8,9},{9,8},{10,11... | collective-permute-start | bytes 589832 | tf_op jit(solution)/shard_map/ppermute | solution.py:14
  45.3 19.9 %collective-permute-start.2 = (f32[2,12,64,64]{3,2,1,0:T(8,128)S(1)}, f32[2,12,64,64]{3,2,1,0:T(8,128)S(1)}, u32[]{:S(2)}, u32[]{:S(2)}) collective-permute-start(f32[2,12,64,64]{3,2,1,0:T(8,128)S(1)} %maximum_select_fusion.3), channel_id=1, source_target_pairs={{0,2},{1,3},{2,0},{3,1},{4,6},{5,7},{6,4},{7,5},{8,10},{9,11},{10,... | collective-permute-start | bytes 1179656 | tf_op jit(solution)/shard_map/ppermute | solution.py:14
  65.5 1.7 copy-start.3
  65.5 36.0 %collective-permute-start.3 = (f32[4,12,64,64]{3,2,1,0:T(8,128)S(1)}, f32[4,12,64,64]{3,2,1,0:T(8,128)}, u32[]{:S(2)}, u32[]{:S(2)}) collective-permute-start(f32[4,12,64,64]{3,2,1,0:T(8,128)S(1)} %maximum_select_fusion.2), channel_id=1, source_target_pairs={{0,4},{1,5},{2,6},{3,7},{4,0},{5,1},{6,2},{7,3},{8,12},{9,13},{10,... | collective-permute-start | bytes 2359304 | tf_op jit(solution)/shard_map/ppermute | solution.py:14
  105.4 137.1 %collective-permute-start.4 = (f32[8,12,64,64]{3,2,1,0:T(8,128)S(1)}, f32[8,12,64,64]{3,2,1,0:T(8,128)}, u32[]{:S(2)}, u32[]{:S(2)}) collective-permute-start(f32[8,12,64,64]{3,2,1,0:T(8,128)S(1)} %maximum_select_fusion.1), channel_id=1, source_target_pairs={{0,8},{1,9},{2,10},{3,11},{4,12},{5,13},{6,14},{7,15},{8,0},{9,1},... | collective-permute-start | bytes 4718600 | tf_op jit(solution)/shard_map/ppermute | solution.py:14
  246.2 6.0 %copy-start.8 = (f32[12,64,64]{2,1,0:T(8,128)S(1)}, f32[12,64,64]{2,1,0:T(8,128)}, u32[]{:S(2)}) copy-start(f32[12,64,64]{2,1,0:T(8,128)} %param.13) | copy-start | bytes 589828
  246.2 6.1 %copy-start.4 = (bf16[2,512,12,64]{1,0,3,2:T(2,128)(2,1)S(1)}, bf16[2,512,12,64]{1,0,3,2:T(2,128)(2,1)}, u32[]{:S(2)}) copy-start(bf16[2,512,12,64]{1,0,3,2:T(2,128)(2,1)} %reshape.64) | copy-start | bytes 4718596
  246.2 6.1 %copy-start.5 = (f32[2,12,64,512]{3,2,1,0:T(8,128)S(1)}, f32[2,12,64,512]{3,2,1,0:T(8,128)}, u32[]{:S(2)}) copy-start(f32[2,12,64,512]{3,2,1,0:T(8,128)} %fusion) | copy-start | bytes 9437188
  246.2 6.1 %copy-start.6 = (f32[2,12,64,64]{3,2,1,0:T(8,128)S(1)}, f32[2,12,64,64]{3,2,1,0:T(8,128)}, u32[]{:S(2)}) copy-start(f32[2,12,64,64]{3,2,1,0:T(8,128)} %reduce-window_subtract_fusion) | copy-start | bytes 1179652
  256.6 0.8 copy-start.9
  257.4 1.3 copy-start.10
  257.4 1.8 copy-start.13
  259.1 5.2 %copy-start.1 = (bf16[768,2304]{1,0:T(8,128)(2,1)S(1)}, bf16[768,2304]{1,0:T(8,128)(2,1)}, u32[]{:S(2)}) copy-start(bf16[768,2304]{1,0:T(8,128)(2,1)} %param.10) | copy-start | bytes 10616836
